TPU v7x, 32 devices: a whole 2x2x4 slice. The times are simulated.
32 devices in a mesh: dp: 4 (over x, core), fsdp: 8 (over z, y).
Axes of the slice: x: 2, y: 2, z: 4, core: 2. Of those that a mesh axis runs over, the one named last changes fastest.
Arguments:
- tokens: bfloat16 [8192, 640], P(('dp', 'fsdp')), may hold values from -6 to 6
- cotangent: bfloat16 [8192, 640], P(('dp', 'fsdp')), may hold values from -6 to 6
- masked_pos: int32 [8192], P(('dp', 'fsdp')), may hold values from 0 to 1
- labels: int32 [8192], P(('dp', 'fsdp')), may hold values from 0 to 3
- decoder: bfloat16 [4, 640], replicated, may hold values from -0.375 to 0.375
- master: float32 [640, 12800], P('fsdp'), may hold values from -0.6324555 to 0.6324555
- small_params: float32 [640, 16], P('fsdp'), may hold values from -0.8 to 1.4
- small_first: float32 [640, 16], P('fsdp'), may hold values from -128 to 128
- small_second: float32 [640, 16], P('fsdp'), may hold values from 163.84 to 4096
- block_slots: int32 [40], replicated, may hold values from 0 to 39, as said below
- first_moment: float32 [40, 640, 320], P('fsdp'), may hold values from -128 to 128
- second_moment: float32 [40, 640, 320], P('fsdp'), may hold values from 163.84 to 4096
- left_bases: float32 [40, 640, 640], P('fsdp'), may hold values from -1 to 1, as said below
- right_bases: float32 [40, 320, 320], P('fsdp'), may hold values from -1 to 1, as said below
Outputs:
- out_tokens: bfloat16 [8192, 640], P(('dp', 'fsdp'))
- grad_tokens: bfloat16 [8192, 640], P(('dp', 'fsdp'))
- grad_weights: float32 [640, 12800], P('fsdp')
- grad_small: float32 [640, 16], P('fsdp')
- new_first: float32 [40, 640, 320], P('fsdp')
- new_second: float32 [40, 640, 320], P('fsdp')
- new_master: float32 [640, 12800], P('fsdp')
- new_copy: bfloat16 [640, 12800], P('fsdp')
- new_small: float32 [640, 16], P('fsdp')
- new_small_first: float32 [640, 16], P('fsdp')
- new_small_second: float32 [640, 16], P('fsdp')
- loss_accuracy: float32 [5], replicated
- counts: int32 [4], replicated
Inputs may be any that keep to these rules, and one draw needn't show every extreme that they name: Distinct slot numbers; block b (columns b * 320 to (b + 1) * 320 - 1 of the weights) keeps its optimizer state in slot block_slots[b], held by fsdp index block_slots[b] // 5; at most 5 blocks on one index. `left_bases`: each slot's matrix is orthogonal. `right_bases`: each slot's matrix is orthogonal.
All inputs are finite; a program needn't handle non-finite values.
Results may differ from a plain program's by a relative error of at most 0.013.
The roundings to bfloat16 on the way count: a program that leaves them out, or rounds other values in their place, can miss the bound.
Values may be sent and summed in bfloat16 or wider, within the bound.
No kernel may reach another device: no remote copies, remote signals or barrier semaphores. Data moves between devices by JAX's collectives and lax.ppermute only.
A program may use at most 256 MiB of HBM per device.

v0:
```python
import jax
import jax.numpy as jnp
from jax import lax
from jax.sharding import PartitionSpec as P

HEAD_DIM = 32
SEQ_LEN = 256
STEP = 5
EPS_NORM = 1e-05
EPS_ADAM = 1e-08
BETA_FIRST = 0.5
BETA_SECOND = 0.5
RATE_MATRIX = 0.02
RATE_VECTOR = 0.05
EXACT_PRECISION = lax.Precision.HIGHEST


def normalize_layer(rows_in, norm_gain, norm_shift):
    centred = rows_in - jnp.mean(rows_in, axis=-1, keepdims=True)
    variance = jnp.mean(centred * centred, axis=-1, keepdims=True)
    return centred * lax.rsqrt(variance + EPS_NORM) * norm_gain + norm_shift


def exact_gelu(inputs):
    return jax.nn.gelu(inputs, approximate=False)


def adam_direction(first_new, second_new):
    return (
        first_new
        / (1.0 - BETA_FIRST**STEP)
        / (jnp.sqrt(second_new / (1.0 - BETA_SECOND**STEP)) + EPS_ADAM)
    )


def contract_rows(left_mat, right_mat):
    return lax.dot_general(
        left_mat, right_mat, (((0,), (0,)), ((), ())), preferred_element_type=jnp.float32
    )


def times_transpose(left_mat, right_mat):
    return lax.dot_general(
        left_mat, right_mat, (((1,), (1,)), ((), ())), preferred_element_type=jnp.float32
    )


def block_scores(queries, key_rows):
    return jnp.einsum(
        "slhd,smhd->shlm", queries, key_rows, preferred_element_type=jnp.float32
    ) * HEAD_DIM ** (-0.5)


def attend_block(weight_blocks):
    queries, key_rows, values = weight_blocks
    scores = block_scores(queries, key_rows)
    highest = jnp.max(scores, axis=-1, keepdims=True)
    exponent = jnp.exp(scores - highest)
    totals = jnp.sum(exponent, axis=-1, keepdims=True)
    weights_soft = (exponent / totals).astype(jnp.bfloat16)
    mixed_rows = jnp.einsum(
        "shlm,smhd->slhd", weights_soft, values, preferred_element_type=jnp.float32
    )
    return (mixed_rows.astype(jnp.bfloat16), (highest + jnp.log(totals))[..., 0])


def attend_back(weight_blocks):
    queries, key_rows, values, log_total, d_attended = weight_blocks
    probabilities = jnp.exp(block_scores(queries, key_rows) - log_total[..., None])
    d_values = jnp.einsum(
        "shlm,slhd->smhd",
        probabilities.astype(jnp.bfloat16),
        d_attended,
        preferred_element_type=jnp.float32,
    )
    d_probs = jnp.einsum("slhd,smhd->shlm", d_attended, values, preferred_element_type=jnp.float32)
    d_scores = (
        probabilities * (d_probs - jnp.sum(probabilities * d_probs, axis=-1, keepdims=True))
    ).astype(jnp.bfloat16)
    d_queries = jnp.einsum(
        "shlm,smhd->slhd", d_scores, key_rows, preferred_element_type=jnp.float32
    ) * HEAD_DIM ** (-0.5)
    d_keys = jnp.einsum(
        "shlm,slhd->smhd", d_scores, queries, preferred_element_type=jnp.float32
    ) * HEAD_DIM ** (-0.5)
    return (
        d_queries.astype(jnp.bfloat16),
        d_keys.astype(jnp.bfloat16),
        d_values.astype(jnp.bfloat16),
    )


def local(
    tokens,
    cotangent,
    masked_pos,
    labels,
    decoder,
    master,
    small_params,
    small_first,
    small_second,
    block_slots,
    first_moment,
    second_moment,
    left_bases,
    right_bases,
):
    model_width = decoder.shape[1]
    hidden = (master.shape[1] - 4 * model_width) // 2
    heads_count = model_width // HEAD_DIM
    token_count = tokens.shape[0]
    local_weights = master.astype(jnp.bfloat16)
    local_small = small_params.astype(jnp.bfloat16)
    weights, small_all = (
        lax.all_gather(local_weights, "fsdp", axis=0, tiled=True),
        lax.all_gather(local_small, "fsdp", axis=0, tiled=True),
    )
    params = small_all.astype(jnp.float32)
    gain_one, shift_one, bias_query, bias_value, bias_output, gain_two, shift_two, bias_down = [
        params[:, column] for column in range(8)
    ]
    bias_up = params[:, 8:].reshape(hidden)
    rows_in = tokens.astype(jnp.float32)
    normed = normalize_layer(rows_in, gain_one, shift_one).astype(jnp.bfloat16)
    bias_qkv = jnp.concatenate([bias_query, jnp.zeros_like(bias_query), bias_value])
    projected = (
        jnp.dot(normed, weights[:, : 3 * model_width], preferred_element_type=jnp.float32)
        + bias_qkv
    ).astype(jnp.bfloat16)
    seq_count = token_count // SEQ_LEN
    per_block = max(1, min(seq_count, 512 // SEQ_LEN))
    block_shape = (seq_count // per_block, per_block, SEQ_LEN, heads_count, HEAD_DIM)
    queries = projected[:, :model_width].reshape(block_shape)
    key_rows = projected[:, model_width : 2 * model_width].reshape(block_shape)
    values = projected[:, 2 * model_width :].reshape(block_shape)
    attention_result, log_total = lax.map(attend_block, (queries, key_rows, values))
    attention_result = attention_result.reshape(token_count, model_width)
    middle = (
        rows_in
        + jnp.dot(
            attention_result,
            weights[:, 3 * model_width : 4 * model_width],
            preferred_element_type=jnp.float32,
        )
        + bias_output
    )
    normed_two = normalize_layer(middle, gain_two, shift_two).astype(jnp.bfloat16)
    pre_active = (
        jnp.dot(
            normed_two,
            weights[:, 4 * model_width : 4 * model_width + hidden],
            preferred_element_type=jnp.float32,
        )
        + bias_up
    )
    active = exact_gelu(pre_active).astype(jnp.bfloat16)
    output_rows = (
        middle + times_transpose(active, weights[:, 4 * model_width + hidden :]) + bias_down
    )
    out_tokens = output_rows.astype(jnp.bfloat16)
    logits = times_transpose(out_tokens, decoder)
    log_norm = jax.nn.logsumexp(logits, axis=-1)
    one_hot = (labels[:, None] == jnp.arange(decoder.shape[0], dtype=jnp.int32)[None, :]).astype(
        jnp.float32
    )
    hidden_tokens = masked_pos.astype(jnp.float32)
    chosen = one_hot * hidden_tokens[:, None]
    entropy = log_norm - jnp.sum(one_hot * logits, axis=-1)
    right_prob = jnp.sum(one_hot * jnp.exp(logits - log_norm[:, None]), axis=-1)
    local_sums = jnp.concatenate(
        [jnp.sum(hidden_tokens * entropy)[None], jnp.sum(chosen * right_prob[:, None], axis=0)]
    )
    global_sums, global_counts = lax.psum((local_sums, jnp.sum(chosen, axis=0)), ("dp", "fsdp"))
    loss_accuracy = jnp.concatenate(
        [
            global_sums[:1] / jnp.maximum(jnp.sum(global_counts), 1.0),
            global_sums[1:] / jnp.maximum(global_counts, 1.0),
        ]
    )
    counts = global_counts.astype(jnp.int32)
    weights_back, small_back = (
        lax.all_gather(local_weights, "fsdp", axis=0, tiled=True),
        lax.all_gather(local_small, "fsdp", axis=0, tiled=True),
    )
    params_back = small_back.astype(jnp.float32)
    back_rows = cotangent.astype(jnp.float32)
    d_active = jnp.dot(
        cotangent, weights_back[:, 4 * model_width + hidden :], preferred_element_type=jnp.float32
    )
    unused, gelu_pull = jax.vjp(exact_gelu, pre_active)
    d_pre = gelu_pull(d_active)[0].astype(jnp.bfloat16)
    d_normed_two = times_transpose(
        d_pre, weights_back[:, 4 * model_width : 4 * model_width + hidden]
    )
    unused, norm_pull_two = jax.vjp(normalize_layer, middle, params_back[:, 5], params_back[:, 6])
    d_middle_norm, d_gain_two, d_shift_two = norm_pull_two(d_normed_two)
    d_middle = back_rows + d_middle_norm
    d_branch = d_middle.astype(jnp.bfloat16)
    d_attended = times_transpose(
        d_branch, weights_back[:, 3 * model_width : 4 * model_width]
    ).astype(jnp.bfloat16)
    d_queries, d_keys, d_values = lax.map(
        attend_back, (queries, key_rows, values, log_total, d_attended.reshape(block_shape))
    )
    d_projected = jnp.concatenate(
        [
            d_queries.reshape(token_count, model_width),
            d_keys.reshape(token_count, model_width),
            d_values.reshape(token_count, model_width),
        ],
        axis=1,
    )
    d_normed = times_transpose(d_projected, weights_back[:, : 3 * model_width])
    unused, norm_pull_one = jax.vjp(normalize_layer, rows_in, params_back[:, 0], params_back[:, 1])
    d_rows_norm, d_gain_one, d_shift_one = norm_pull_one(d_normed)
    grad_tokens = (d_middle + d_rows_norm).astype(jnp.bfloat16)
    grad_w_local = jnp.concatenate(
        [
            contract_rows(normed, d_projected),
            contract_rows(attention_result, d_branch),
            contract_rows(normed_two, d_pre),
            contract_rows(cotangent, active),
        ],
        axis=1,
    )
    proj_sums = jnp.sum(d_projected.astype(jnp.float32), axis=0)
    small_cols = jnp.stack(
        [
            d_gain_one,
            d_shift_one,
            proj_sums[:model_width],
            proj_sums[2 * model_width :],
            jnp.sum(d_branch.astype(jnp.float32), axis=0),
            d_gain_two,
            d_shift_two,
            jnp.sum(back_rows, axis=0),
        ],
        axis=1,
    )
    grad_s_local = jnp.concatenate(
        [small_cols, jnp.sum(d_pre.astype(jnp.float32), axis=0).reshape(model_width, -1)], axis=1
    )
    part_w, part_s = (
        lax.psum_scatter(grad_w_local, "dp", scatter_dimension=1, tiled=True),
        lax.psum_scatter(grad_s_local, "dp", scatter_dimension=1, tiled=True),
    )
    part_w, part_s = (
        lax.psum_scatter(part_w, "fsdp", scatter_dimension=0, tiled=True),
        lax.psum_scatter(part_s, "fsdp", scatter_dimension=0, tiled=True),
    )
    grad_w, grad_s = (
        lax.all_gather(part_w, "dp", axis=1, tiled=True),
        lax.all_gather(part_s, "dp", axis=1, tiled=True),
    )
    row_count = grad_w.shape[0]
    block_width = model_width // 2
    block_count = grad_w.shape[1] // block_width
    owned_slots = first_moment.shape[0]
    devices = lax.axis_size("fsdp")
    slot_ids = jnp.arange(owned_slots * devices, dtype=jnp.int32)
    matches = block_slots[None, :] == slot_ids[:, None]
    in_use = jnp.any(matches, axis=1)
    source_block = jnp.sum(
        jnp.where(matches, jnp.arange(block_count, dtype=jnp.int32)[None, :], 0), axis=1
    )
    outgoing = jnp.take(grad_w.reshape(row_count, block_count, block_width), source_block, axis=1)
    outgoing = jnp.where(in_use[None, :, None], outgoing, 0.0).reshape(
        row_count, devices, owned_slots, block_width
    )
    incoming = lax.all_to_all(outgoing, "fsdp", split_axis=1, concat_axis=0, tiled=True).reshape(
        row_count * devices, owned_slots, block_width
    )
    my_use = lax.dynamic_slice_in_dim(in_use, lax.axis_index("fsdp") * owned_slots, owned_slots)
    eigen_turned = jnp.einsum("kdi,dkc->kic", left_bases, incoming, precision=EXACT_PRECISION)
    eigen_turned = jnp.einsum("kic,kcj->kij", eigen_turned, right_bases, precision=EXACT_PRECISION)
    first_new = BETA_FIRST * first_moment + (1.0 - BETA_FIRST) * eigen_turned
    second_new = BETA_SECOND * second_moment + (1.0 - BETA_SECOND) * eigen_turned * eigen_turned
    direction = adam_direction(first_new, second_new)
    rotated_gradient = jnp.einsum("kij,klj->kil", direction, right_bases, precision=EXACT_PRECISION)
    rotated_gradient = jnp.einsum(
        "kdi,kil->dkl", left_bases, rotated_gradient, precision=EXACT_PRECISION
    )
    returned = lax.all_to_all(
        rotated_gradient.reshape(devices, row_count, owned_slots, block_width),
        "fsdp",
        split_axis=0,
        concat_axis=0,
        tiled=True,
    )
    by_slot = jnp.moveaxis(returned, 1, 0).reshape(row_count, devices * owned_slots, block_width)
    update = jnp.take(by_slot, block_slots, axis=1).reshape(row_count, block_count * block_width)
    new_master = master - RATE_MATRIX * update
    new_copy = new_master.astype(jnp.bfloat16)
    keep_slot = my_use[:, None, None]
    new_first = jnp.where(keep_slot, first_new, 0.0)
    new_second = jnp.where(keep_slot, second_new, 0.0)
    new_small_first = BETA_FIRST * small_first + (1.0 - BETA_FIRST) * grad_s
    new_small_second = BETA_SECOND * small_second + (1.0 - BETA_SECOND) * grad_s * grad_s
    new_small = small_params - RATE_VECTOR * adam_direction(new_small_first, new_small_second)
    return (
        out_tokens,
        grad_tokens,
        grad_w,
        grad_s,
        new_first,
        new_second,
        new_master,
        new_copy,
        new_small,
        new_small_first,
        new_small_second,
        loss_accuracy,
        counts,
    )


def solution(mesh):
    return jax.shard_map(
        local,
        mesh=mesh,
        in_specs=(
            P(("dp", "fsdp"), None),
            P(("dp", "fsdp"), None),
            P(("dp", "fsdp")),
            P(("dp", "fsdp")),
            P(),
            P("fsdp", None),
            P("fsdp", None),
            P("fsdp", None),
            P("fsdp", None),
            P(),
            P("fsdp", None, None),
            P("fsdp", None, None),
            P("fsdp", None, None),
            P("fsdp", None, None),
        ),
        out_specs=(
            P(("dp", "fsdp"), None),
            P(("dp", "fsdp"), None),
            P("fsdp", None),
            P("fsdp", None),
            P("fsdp", None, None),
            P("fsdp", None, None),
            P("fsdp", None),
            P("fsdp", None),
            P("fsdp", None),
            P("fsdp", None),
            P("fsdp", None),
            P(),
            P(),
        ),
        check_vma=False,
    )
```

profile of v0, /device:TPU:0, one launch (start us, length us, event | category | flops | bytes accessed | tf_op | source)
XLA Modules:
  0.0 1169.3 jit_solution(2485766205392647652)
XLA Ops:
  7.3 3.8 convert_element_type.121
  11.2 33.4 %all-gather = bf16[8,80,16]{1,2,0:T(8,128)(2,1)S(1)} all-gather(bf16[1,80,16]{1,2,0:T(8,128)(2,1)S(1)} %convert_bitcast_fusion), channel_id=1, replica_groups=mesh['dp'=4,'fsdp'=8] {'fsdp'}, dimensions={0}, use_global_device_ids=true | all-gather | bytes 23040 | tf_op jit(solution)/shard_map/all_gather | solution.py:117
  46.0 190.6 %all-gather.5.cloned.1.call-done = bf16[640,12800]{1,0:T(8,128)(2,1)} async-done(((bf16[80,12800]{1,0:T(8,128)(2,1)}), bf16[640,12800]{1,0:T(8,128)(2,1)}) %all-gather.5.cloned.1.call-update) | async-done | bytes 16384016 | tf_op jit(solution)/shard_map/all_gather | solution.py:116
  236.6 2.8 fusion.29
  239.4 0.9 fusion.87
  240.5 1.3 copy.111
  241.8 2.0 copy.110
  243.8 0.9 multiply_reduce_fusion.1
  244.7 0.9 fusion.15
  245.7 1.1 fusion.45
  247.3 1.9 slice-done.3
  249.2 1.4 slice-done.4
  250.6 1.1 slice-done.5
  252.5 15.0 %multiply_convert_fusion.1 = (bf16[256,5120]{1,0:T(8,128)(2,1)}, f32[256,5120]{1,0:T(8,128)}, f32[256,5120]{1,0:T(8,128)}) fusion(f32[5120]{0:T(1024)S(1)} %add.172, bf16[640,12800]{1,0:T(8,128)(2,1)S(1)} %bitcast.115, f32[256,640]{1,0:T(8,128)S(1)} %get-tuple-element.106, f32[640]{0:T(1024)S(1)} %get-tuple-element.67, f32[640]{0:T(1024)S(1)} %get-tuple-element.68, ...), kind=kOutput, calls=%fused_computation.21 | convolution fusion | flops 1765048320 | bytes 20346880 | tf_op jit(solution)/shard_map/dot_general | solution.py:150
  267.5 6.6 convert_reduce_fusion
  274.1 2.4 multiply_reduce_fusion.2
  276.9 0.9 copy-done.6
  278.0 1.6 fusion.92
  279.5 1.2 convolution_convert_fusion
  280.7 1.9 copy.115
  282.6 3.7 fusion.48
  286.9 1.4 multiply_reduce_fusion
  288.3 1.4 multiply_convert_fusion
  291.4 6.7 fusion.80
  298.1 6.6 convolution_bitcast_fusion
  304.7 3.3 fusion.76
  308.0 21.8 %pad_maximum_fusion = f32[640,12800]{1,0:T(8,128)} fusion(f32[640,5120]{1,0:T(8,128)} %convolution_bitcast_fusion, f32[640,5120]{1,0:T(8,128)} %fusion.80, f32[640,640]{1,0:T(8,128)S(1)} %copy-done.5, f32[640,1920]{1,0:T(8,128)} %fusion.76), kind=kLoop, calls=%fused_computation.2 | loop fusion | flops 24576000 | bytes 65536000 | tf_op jit(solution)/shard_map/concatenate | solution.py:218
  329.9 225.7 %reduce-scatter.5.cloned.1.call-done = f32[640,3200]{1,0:T(8,128)} async-done(((f32[640,12800]{1,0:T(8,128)}), f32[640,3200]{1,0:T(8,128)}) %reduce-scatter.5.cloned.1.call-update) | async-done | bytes 8192016 | tf_op jit(solution)/shard_map/reduce_scatter | solution.py:245
  555.7 149.0 %reduce-scatter.7.cloned.1.call-done = f32[80,3200]{1,0:T(8,128)} async-done(((f32[640,3200]{1,0:T(8,128)}), f32[80,3200]{1,0:T(8,128)}) %reduce-scatter.7.cloned.1.call-update) | async-done | bytes 1024016 | tf_op jit(solution)/shard_map/reduce_scatter | solution.py:249
  705.0 34.2 %all-gather.7.cloned.1.call-done = f32[80,12800]{1,0:T(8,128)} async-done(((f32[80,3200]{1,0:T(8,128)}), f32[80,12800]{1,0:T(8,128)}) %all-gather.7.cloned.1.call-update) | async-done | bytes 4096016 | tf_op jit(solution)/shard_map/all_gather | solution.py:253
  739.2 5.7 reshape.267
  744.9 5.5 copy.130
  750.4 5.5 gather_fusion
  755.9 5.6 bitcast_select_fusion
  761.6 5.5 all-to-all-start
  767.1 109.1 %all-to-all-done = f32[80,8,5,320]{3,0,2,1:T(8,128)} async-done(((f32[80,8,5,320]{3,0,2,1:T(8,128)}), f32[80,8,5,320]{3,0,2,1:T(8,128)}, u32[]{:S(2)}, u32[]{:S(2)}) %all-to-all-start) | async-done | bytes 4096032 | tf_op jit(solution)/shard_map/all_to_all | solution.py:271
  876.2 2.8 copy.131
  879.0 33.4 %fusion.93 = f32[5,320,640]{2,1,0:T(8,128)S(1)} fusion(f32[640,5,320]{2,0,1:T(8,128)S(1)} %bitcast.89, f32[5,640,640]{2,1,0:T(8,128)} %param.28), kind=kOutput, calls=%fused_computation.168 | convolution fusion | flops 7864320000 | bytes 16384000 | tf_op jit(solution)/shard_map/kdi,dkc->kic/dot_general | solution.py:275
  912.4 18.5 %broadcast_select_fusion = (f32[5,640,320]{1,2,0:T(8,128)}, f32[5,640,320]{1,2,0:T(8,128)}, f32[5,640,320]{1,2,0:T(8,128)}) fusion(pred[5]{0:T(512)(128)(4,1)S(1)} %dynamic_slice.21, f32[5,640,320]{1,2,0:T(8,128)} %param.27, f32[5,640,320]{1,2,0:T(8,128)} %param.26, f32[5,320,640]{2,1,0:T(8,128)S(1)} %fusion.93, f32[5,320,320]{2,1,0:T(8,128)S(1)} %copy-done), kind=kOutput, calls=%fused_computation.61 | convolution fusion | flops 3940352000 | bytes 26624004 | tf_op jit(solution)/shard_map/kic,kcj->kij/dot_general | solution.py:276
  930.9 19.0 %fusion.17 = f32[5,640,320]{1,2,0:T(8,128)S(1)} fusion(f32[5,320,320]{2,1,0:T(8,128)S(1)} %copy-done, f32[5,640,320]{1,2,0:T(8,128)} %get-tuple-element.114, f32[5,640,320]{1,2,0:T(8,128)} %param.26, f32[5,640,320]{1,2,0:T(8,128)} %param.27), kind=kOutput, calls=%fused_computation.42 | convolution fusion | flops 3942400000 | bytes 18432000 | tf_op jit(solution)/shard_map/kij,klj->kil/dot_general | solution.py:280
  950.0 20.1 %convolution_bitcast_fusion.1 = f32[640,5,320]{0,2,1:T(8,128)} fusion(f32[5,640,320]{1,2,0:T(8,128)S(1)} %fusion.17, f32[5,640,640]{2,1,0:T(8,128)S(1)} %bitcast.87), kind=kOutput, calls=%fused_computation.58 | convolution fusion | flops 7864320000 | bytes 16384000 | tf_op jit(solution)/shard_map/kdi,kil->dkl/dot_general | solution.py:281
  970.2 6.6 copy.134
  976.7 4.9 copy.135
  981.7 4.7 all-to-all-start.1
  988.0 0.9 reshape.266
  989.8 0.9 stack.38
  991.6 1.6 convert_reduce_fusion.1
  994.0 3.1 fusion.81
  997.6 1.1 convert_reduce_fusion.3
  998.8 0.9 stack.39
  1002.3 2.3 concatenate.21
  1004.6 15.0 %all-reduce = f32[640,16]{1,0:T(8,128)} all-reduce(f32[640,16]{1,0:T(8,128)S(1)} %concatenate.21), channel_id=4, replica_groups=mesh['dp'=4,'fsdp'=8] {'dp'}, use_global_device_ids=true, to_apply=%region_21.22.clone | all-reduce | flops 10240 | bytes 81920
  1019.6 1.8 constant_dynamic-slice_fusion
  1021.5 5.9 fusion.42
  1029.3 88.3 %all-reduce.1 = (f32[4]{0:T(128)S(1)}, f32[5]{0:T(128)S(1)}) all-reduce(f32[4]{0:T(128)S(1)} %get-tuple-element.77, f32[5]{0:T(128)S(1)} %pad_maximum_fusion.3), channel_id=1, replica_groups=mesh['dp'=4,'fsdp'=8] {'dp','fsdp'}, use_global_device_ids=true, to_apply=%region_33.35 | all-reduce | flops 9 | bytes 72 | tf_op jit(solution)/shard_map/psum | solution.py:174
  1117.6 1.1 fusion.89
  1120.0 8.9 reduce-scatter.9.cloned.1.call-done
  1129.7 5.2 all-gather.1
  1135.5 5.5 gather_fusion.1
  1141.0 3.0 bitcast_multiply_fusion
  1144.1 3.7 copy.136
  1147.8 5.5 mul.298
  1153.3 6.7 fusion.83
  1160.0 2.0 copy.148
  (153 shorter events, 17.4 us)
Async XLA Ops:
  7.2 905.2 %copy-start = (f32[5,320,320]{2,1,0:T(8,128)S(1)}, f32[5,320,320]{2,1,0:T(8,128)}, u32[]{:S(2)}) copy-start(f32[5,320,320]{2,1,0:T(8,128)} %param.29) | copy-start | bytes 6144004
  7.2 4.0 copy-start.25
  7.2 38.5 %copy-start.4 = (bf16[256,640]{1,0:T(8,128)(2,1)S(1)}, bf16[256,640]{1,0:T(8,128)(2,1)}, u32[]{:S(2)}) copy-start(bf16[256,640]{1,0:T(8,128)(2,1)} %param.16) | copy-start | bytes 983044
  7.2 229.4 %all-gather.5.cloned.1.call-start = ((), (), s32[]{:S(2)}) async-start(), calls=%async_computation.5 | async-start | bytes 18432000 | tf_op jit(solution)/shard_map/all_gather | solution.py:116
  11.1 544.6 %reduce-scatter.5.cloned.1.call-start = ((), (), s32[]{:S(2)}) async-start(), calls=%async_computation.6 | async-start | bytes 40960000 | tf_op jit(solution)/shard_map/reduce_scatter | solution.py:245
  46.0 198.6 %copy-start.27 = (f32[256]{0:T(256)}, f32[256]{0:T(256)S(1)}, u32[]{:S(2)}) copy-start(f32[256]{0:T(256)S(1)} %fusion.63) | copy-start | bytes 3076
  240.5 5.1 copy-start.12
  241.7 3.9 copy-start.14
  243.8 1.9 copy-start.22
  243.8 3.6 slice-start.2
  244.7 2.7 copy-start.1
  244.7 4.5 slice-start.3
  245.6 4.9 slice-start.4
  245.7 6.0 slice-start.5
  252.5 15.0 %copy-start.16 = (bf16[256,640]{1,0:T(8,128)(2,1)S(1)}, bf16[256,640]{1,0:T(8,128)(2,1)}, u32[]{:S(2)}) copy-start(bf16[256,640]{1,0:T(8,128)(2,1)} %param.17) | copy-start | bytes 983044
  274.1 2.4 copy-start.19
  276.9 0.9 copy-start.6
  282.6 4.1 copy-start.2
  282.6 4.2 copy-start.9
  282.6 4.3 copy-start.23
  286.9 17.8 %copy-start.8 = (bf16[20,32,256]{2,1,0:T(8,128)(2,1)}, bf16[20,32,256]{2,1,0:T(8,128)(2,1)S(1)}, u32[]{:S(2)}) copy-start(bf16[20,32,256]{2,1,0:T(8,128)(2,1)S(1)} %fusion.48) | copy-start | bytes 983044
  288.2 1.4 copy-start.15
  288.2 2.3 copy-start.13
  289.7 1.7 copy-start.20
  290.6 14.1 %copy-start.10 = (bf16[20,32,256]{2,1,0:T(8,128)(2,1)}, bf16[20,32,256]{2,1,0:T(8,128)(2,1)S(1)}, u32[]{:S(2)}) copy-start(bf16[20,32,256]{2,1,0:T(8,128)(2,1)S(1)} %fusion.47) | copy-start | bytes 983044
  291.4 13.3 %copy-start.11 = (bf16[20,32,256]{2,1,0:T(8,128)(2,1)}, bf16[20,32,256]{2,1,0:T(8,128)(2,1)S(1)}, u32[]{:S(2)}) copy-start(bf16[20,32,256]{2,1,0:T(8,128)(2,1)S(1)} %fusion.46) | copy-start | bytes 983044
  291.4 6.7 copy-start.17
  291.4 6.7 copy-start.21
  304.7 3.3 copy-start.5
  329.9 374.9 %copy-start.35 = (s32[40]{0:T(128)S(1)}, s32[40]{0:T(128)}, u32[]{:S(2)}) copy-start(s32[40]{0:T(128)} %param.25) | copy-start | bytes 484
  329.9 374.8 %reduce-scatter.7.cloned.1.call-start = ((), (), s32[]{:S(2)}) async-start(), calls=%async_computation.7 | async-start | bytes 9216000 | tf_op jit(solution)/shard_map/reduce_scatter | solution.py:249
  555.7 183.5 %all-gather.7.cloned.1.call-start = ((), (), s32[]{:S(2)}) async-start(), calls=%async_computation.8 | async-start | bytes 5120000 | tf_op jit(solution)/shard_map/all_gather | solution.py:253
  761.6 114.7 %all-to-all-start = ((f32[80,8,5,320]{3,0,2,1:T(8,128)}), f32[80,8,5,320]{3,0,2,1:T(8,128)}, u32[]{:S(2)}, u32[]{:S(2)}) async-start(f32[80,8,5,320]{3,0,2,1:T(8,128)} %bitcast.88), calls=%async_computation.3 | async-start | bytes 9830400 | tf_op jit(solution)/shard_map/all_to_all | solution.py:271
  879.0 71.0 %slice-start = ((s8[8192000]{0:T(1024)(128)(4,1)}), s8[4194304]{0:T(1024)(128)(4,1)S(1)}, s32[]{:S(2)}) async-start(s8[8192000]{0:T(1024)(128)(4,1)} %bitcast.86), calls=%async_computation.10 | async-start | bytes 8388608
  912.4 37.6 %slice-start.1 = ((s8[8192000]{0:T(1024)(128)(4,1)}), s8[3997696]{0:T(1024)(128)(4,1)S(1)}, s32[]{:S(2)}) async-start(s8[8192000]{0:T(1024)(128)(4,1)} %bitcast.86), calls=%async_computation.11 | async-start | bytes 7995392
  981.7 5.0 copy-start.32
  981.7 5.0 copy-start.36
  981.7 153.8 %all-to-all-start.1 = ((f32[8,80,5,320]{3,1,2,0:T(8,128)}), f32[8,80,5,320]{3,1,2,0:T(8,128)}, u32[]{:S(2)}, u32[]{:S(2)}) async-start(f32[8,80,5,320]{3,1,2,0:T(8,128)} %copy.135), calls=%async_computation.4 | async-start | bytes 9830400 | tf_op jit(solution)/shard_map/all_to_all | solution.py:284
  986.4 142.4 %reduce-scatter.9.cloned.1.call-start = ((), (), s32[]{:S(2)}) async-start(), calls=%async_computation.9 | async-start | bytes 368640 | tf_op jit(solution)/shard_map/reduce_scatter | solution.py:250
  988.9 8.3 copy-start.28
  991.6 6.1 copy-start.7
  991.6 6.1 copy-start.18
  997.2 24.3 %copy-start.34 = (f32[640]{0:T(1024)S(1)}, f32[640]{0:T(1024)}, u32[]{:S(2)}) copy-start(f32[640]{0:T(1024)} %get-tuple-element.66) | copy-start | bytes 7684
  1021.5 6.0 copy-start.31
  1021.5 6.3 copy-start.33
  1021.5 113.4 %copy-start.26 = (f32[80,16]{0,1:T(8,128)S(1)}, f32[80,16]{0,1:T(8,128)}, u32[]{:S(2)}) copy-start(f32[80,16]{0,1:T(8,128)} %param.22) | copy-start | bytes 15364
  1021.5 113.4 %copy-start.29 = (f32[80,16]{0,1:T(8,128)S(1)}, f32[80,16]{0,1:T(8,128)}, u32[]{:S(2)}) copy-start(f32[80,16]{0,1:T(8,128)} %param.23) | copy-start | bytes 15364
  1021.5 113.4 %copy-start.30 = (f32[80,16]{0,1:T(8,128)S(1)}, f32[80,16]{0,1:T(8,128)}, u32[]{:S(2)}) copy-start(f32[80,16]{0,1:T(8,128)} %param.24) | copy-start | bytes 15364
  1027.5 116.6 %copy-start.24 = (bf16[256,640]{1,0:T(8,128)(2,1)}, bf16[256,640]{1,0:T(8,128)(2,1)S(1)}, u32[]{:S(2)}) copy-start(bf16[256,640]{1,0:T(8,128)(2,1)S(1)} %fusion.42) | copy-start | bytes 983044
  1153.3 6.7 copy-start.3
Sparse Core Ops, SparseCore 0:
  11.2 225.3 all-gather.4
  330.0 225.6 reduce-scatter.4
  559.4 145.2 reduce-scatter.6
  706.1 32.9 all-gather.6
  1021.6 107.2 reduce-scatter.8
where the time goes:
time: 1180 us; the launch traced here: 1170 us
  waiting for transfers between devices  717 us (61%)
  matrix products  156 us (13%)
  blocking collectives  142 us (12%)
  local copies, waits for them, and re-layouts  76.1 us (6%)
  other arithmetic  51.6 us (4%)
  between operations  16 us (1%)
    reduce_scatter x1, waiting for transfers between devices, local(): lax.psum_scatter(grad_w_local, 'dp', scatter_dimension=1, tiled=True)  226 us
    all_gather x1, waiting for transfers between devices, local(): lax.all_gather(local_weights, 'fsdp', axis=0, tiled=True)  191 us
    reduce_scatter x1, waiting for transfers between devices, local(): lax.psum_scatter(part_w, 'fsdp', scatter_dimension=0, tiled=True)  149 us
    all_to_all x1, waiting for transfers between devices, local(): lax.all_to_all(outgoing, 'fsdp', split_axis=1, concat_axis=0, tiled=True)  109 us
    psum x1, blocking collectives, local(): lax.psum((local_sums, jnp.sum(chosen, axis=0)), ('dp', 'fsdp'))  88.3 us
    all_gather x1, waiting for transfers between devices, local(): lax.all_gather(part_w, 'dp', axis=1, tiled=True)  34.2 us
    all_gather x1, blocking collectives, local(): lax.all_gather(local_small, 'fsdp', axis=0, tiled=True)  33.4 us
    dot_general x1, matrix products, local(): jnp.einsum('kdi,dkc->kic', left_bases, incoming, precision=EXACT_PRECISION)  33.4 us
  transfers between devices with their start and end apart: 7, of which 6 were waited for; matrix products, arithmetic and copies ran while one was open for 3% of the time, Pallas kernels for 0%

commit v1 on v0

--- a/solution.py
+++ b/solution.py
@@ -268,9 +268,10 @@
     outgoing = jnp.where(in_use[None, :, None], outgoing, 0.0).reshape(
         row_count, devices, owned_slots, block_width
     )
-    incoming = lax.all_to_all(outgoing, "fsdp", split_axis=1, concat_axis=0, tiled=True).reshape(
-        row_count * devices, owned_slots, block_width
-    )
+    incoming = jnp.concatenate(
+        lax.all_to_all(jnp.stack(jnp.split(outgoing, lax.axis_size("fsdp"), axis=1)), "fsdp", 0, 0),
+        axis=0,
+    ).reshape(row_count * devices, owned_slots, block_width)
     my_use = lax.dynamic_slice_in_dim(in_use, lax.axis_index("fsdp") * owned_slots, owned_slots)
     eigen_turned = jnp.einsum("kdi,dkc->kic", left_bases, incoming, precision=EXACT_PRECISION)
     eigen_turned = jnp.einsum("kic,kcj->kij", eigen_turned, right_bases, precision=EXACT_PRECISION)

time: 1180 us -> 1180 us (level)
  no operation moved by 1% of the time
where the time goes in v1:
time: 1180 us; the launch traced here: 1170 us
  waiting for transfers between devices  717 us (61%)
  matrix products  156 us (13%)
  blocking collectives  142 us (12%)
  local copies, waits for them, and re-layouts  83.2 us (7%)
  other arithmetic  49.4 us (4%)
  between operations  16.1 us (1%)
    reduce_scatter x1, waiting for transfers between devices, local(): lax.psum_scatter(grad_w_local, 'dp', scatter_dimension=1, tiled=True)  226 us
    all_gather x1, waiting for transfers between devices, local(): lax.all_gather(local_weights, 'fsdp', axis=0, tiled=True)  191 us
    reduce_scatter x1, waiting for transfers between devices, local(): lax.psum_scatter(part_w, 'fsdp', scatter_dimension=0, tiled=True)  149 us
    all_to_all x1, waiting for transfers between devices, local(): lax.all_to_all(jnp.stack(jnp.split(outgoing, lax.axis_size('fsdp'), axis=...  109 us
    psum x1, blocking collectives, local(): lax.psum((local_sums, jnp.sum(chosen, axis=0)), ('dp', 'fsdp'))  88.3 us
    all_gather x1, waiting for transfers between devices, local(): lax.all_gather(part_w, 'dp', axis=1, tiled=True)  34.2 us
    all_gather x1, blocking collectives, local(): lax.all_gather(local_small, 'fsdp', axis=0, tiled=True)  33.4 us
    dot_general x1, matrix products, local(): jnp.einsum('kdi,dkc->kic', left_bases, incoming, precision=EXACT_PRECISION)  33.4 us
  transfers between devices with their start and end apart: 7, of which 6 were waited for; matrix products, arithmetic and copies ran while one was open for 3% of the time, Pallas kernels for 0%

profile of v1, /device:TPU:0, one launch (start us, length us, event | category | flops | bytes accessed | tf_op | source)
XLA Modules:
  0.0 1174.1 jit_solution(5509462171209980996)
XLA Ops:
  7.3 3.8 convert_element_type.121
  11.2 33.4 %all-gather = bf16[8,80,16]{1,2,0:T(8,128)(2,1)S(1)} all-gather(bf16[1,80,16]{1,2,0:T(8,128)(2,1)S(1)} %convert_bitcast_fusion), channel_id=1, replica_groups=mesh['dp'=4,'fsdp'=8] {'fsdp'}, dimensions={0}, use_global_device_ids=true | all-gather | bytes 23040 | tf_op jit(solution)/shard_map/all_gather | solution.py:117
  46.0 190.6 %all-gather.5.cloned.1.call-done = bf16[640,12800]{1,0:T(8,128)(2,1)} async-done(((bf16[80,12800]{1,0:T(8,128)(2,1)}), bf16[640,12800]{1,0:T(8,128)(2,1)}) %all-gather.5.cloned.1.call-update) | async-done | bytes 16384016 | tf_op jit(solution)/shard_map/all_gather | solution.py:116
  236.6 2.8 fusion.29
  239.4 0.9 fusion.95
  240.5 1.3 copy.117
  241.8 2.0 copy.116
  243.8 0.9 multiply_reduce_fusion.1
  244.7 0.9 fusion.15
  245.7 1.1 fusion.45
  247.3 1.9 slice-done.3
  249.2 1.4 slice-done.4
  250.6 1.1 slice-done.5
  252.5 15.0 %multiply_convert_fusion.1 = (bf16[256,5120]{1,0:T(8,128)(2,1)}, f32[256,5120]{1,0:T(8,128)}, f32[256,5120]{1,0:T(8,128)}) fusion(f32[5120]{0:T(1024)S(1)} %add.172, bf16[640,12800]{1,0:T(8,128)(2,1)S(1)} %bitcast.151, f32[256,640]{1,0:T(8,128)S(1)} %get-tuple-element.106, f32[640]{0:T(1024)S(1)} %get-tuple-element.67, f32[640]{0:T(1024)S(1)} %get-tuple-element.68, ...), kind=kOutput, calls=%fused_computation.21 | convolution fusion | flops 1765048320 | bytes 20346880 | tf_op jit(solution)/shard_map/dot_general | solution.py:150
  267.5 6.6 convert_reduce_fusion
  274.1 2.4 multiply_reduce_fusion.2
  278.0 1.6 fusion.100
  279.5 1.2 convolution_convert_fusion
  280.7 1.9 copy.121
  282.6 3.7 fusion.48
  286.9 1.4 multiply_reduce_fusion
  288.3 1.4 multiply_convert_fusion
  291.4 6.7 fusion.88
  298.1 6.6 convolution_bitcast_fusion
  304.7 3.3 fusion.84
  308.0 21.8 %pad_maximum_fusion = f32[640,12800]{1,0:T(8,128)} fusion(f32[640,5120]{1,0:T(8,128)} %convolution_bitcast_fusion, f32[640,5120]{1,0:T(8,128)} %fusion.88, f32[640,640]{1,0:T(8,128)S(1)} %copy-done.5, f32[640,1920]{1,0:T(8,128)} %fusion.84), kind=kLoop, calls=%fused_computation.2 | loop fusion | flops 24576000 | bytes 65536000 | tf_op jit(solution)/shard_map/concatenate | solution.py:218
  329.9 225.7 %reduce-scatter.5.cloned.1.call-done = f32[640,3200]{1,0:T(8,128)} async-done(((f32[640,12800]{1,0:T(8,128)}), f32[640,3200]{1,0:T(8,128)}) %reduce-scatter.5.cloned.1.call-update) | async-done | bytes 8192016 | tf_op jit(solution)/shard_map/reduce_scatter | solution.py:245
  555.7 149.0 %reduce-scatter.7.cloned.1.call-done = f32[80,3200]{1,0:T(8,128)} async-done(((f32[640,3200]{1,0:T(8,128)}), f32[80,3200]{1,0:T(8,128)}) %reduce-scatter.7.cloned.1.call-update) | async-done | bytes 1024016 | tf_op jit(solution)/shard_map/reduce_scatter | solution.py:249
  705.0 34.2 %all-gather.7.cloned.1.call-done = f32[80,12800]{1,0:T(8,128)} async-done(((f32[80,3200]{1,0:T(8,128)}), f32[80,12800]{1,0:T(8,128)}) %all-gather.7.cloned.1.call-update) | async-done | bytes 4096016 | tf_op jit(solution)/shard_map/all_gather | solution.py:253
  739.2 5.7 reshape.263
  744.9 5.5 copy.136
  750.4 5.5 gather_fusion
  755.9 3.4 bitcast_select_fusion
  763.7 0.9 fusion.67
  764.6 0.9 fusion.66
  766.4 5.5 all-to-all-start
  772.0 109.1 %all-to-all-done = f32[8,80,1,5,320]{4,1,3,2,0:T(8,128)} async-done(((f32[8,80,1,5,320]{4,1,3,2,0:T(8,128)}), f32[8,80,1,5,320]{4,1,3,2,0:T(8,128)}, u32[]{:S(2)}, u32[]{:S(2)}) %all-to-all-start) | async-done | bytes 4096032 | tf_op jit(solution)/shard_map/all_to_all | solution.py:272
  881.1 2.8 copy.137
  883.9 33.4 %fusion.101 = f32[5,320,640]{2,1,0:T(8,128)S(1)} fusion(f32[640,5,320]{2,0,1:T(8,128)S(1)} %bitcast.125, f32[5,640,640]{2,1,0:T(8,128)} %param.28), kind=kOutput, calls=%fused_computation.184 | convolution fusion | flops 7864320000 | bytes 16384000 | tf_op jit(solution)/shard_map/kdi,dkc->kic/dot_general | solution.py:276
  917.3 18.5 %broadcast_select_fusion = (f32[5,640,320]{1,2,0:T(8,128)}, f32[5,640,320]{1,2,0:T(8,128)}, f32[5,640,320]{1,2,0:T(8,128)}) fusion(pred[5]{0:T(512)(128)(4,1)S(1)} %dynamic_slice.21, f32[5,640,320]{1,2,0:T(8,128)} %param.27, f32[5,640,320]{1,2,0:T(8,128)} %param.26, f32[5,320,640]{2,1,0:T(8,128)S(1)} %fusion.101, f32[5,320,320]{2,1,0:T(8,128)S(1)} %copy-done), kind=kOutput, calls=%fused_computation.61 | convolution fusion | flops 3940352000 | bytes 26624004 | tf_op jit(solution)/shard_map/kic,kcj->kij/dot_general | solution.py:277
  935.8 19.0 %fusion.17 = f32[5,640,320]{1,2,0:T(8,128)S(1)} fusion(f32[5,320,320]{2,1,0:T(8,128)S(1)} %copy-done, f32[5,640,320]{1,2,0:T(8,128)} %get-tuple-element.114, f32[5,640,320]{1,2,0:T(8,128)} %param.26, f32[5,640,320]{1,2,0:T(8,128)} %param.27), kind=kOutput, calls=%fused_computation.42 | convolution fusion | flops 3942400000 | bytes 18432000 | tf_op jit(solution)/shard_map/kij,klj->kil/dot_general | solution.py:281
  954.9 20.1 %convolution_bitcast_fusion.1 = f32[640,5,320]{0,2,1:T(8,128)} fusion(f32[5,640,320]{1,2,0:T(8,128)S(1)} %fusion.17, f32[5,640,640]{2,1,0:T(8,128)S(1)} %bitcast.116), kind=kOutput, calls=%fused_computation.58 | convolution fusion | flops 7864320000 | bytes 16384000 | tf_op jit(solution)/shard_map/kdi,kil->dkl/dot_general | solution.py:282
  975.0 6.6 copy.140
  981.6 4.9 copy.141
  986.5 4.7 all-to-all-start.1
  992.8 0.9 reshape.262
  994.6 0.9 stack.74
  996.4 1.6 convert_reduce_fusion.1
  998.9 3.1 fusion.89
  1002.5 1.1 convert_reduce_fusion.3
  1007.1 2.3 concatenate.21
  1009.4 15.0 %all-reduce = f32[640,16]{1,0:T(8,128)} all-reduce(f32[640,16]{1,0:T(8,128)S(1)} %concatenate.21), channel_id=4, replica_groups=mesh['dp'=4,'fsdp'=8] {'dp'}, use_global_device_ids=true, to_apply=%region_21.22.clone | all-reduce | flops 10240 | bytes 81920
  1024.4 1.8 constant_dynamic-slice_fusion
  1026.4 5.9 fusion.42
  1034.1 88.3 %all-reduce.1 = (f32[4]{0:T(128)S(1)}, f32[5]{0:T(128)S(1)}) all-reduce(f32[4]{0:T(128)S(1)} %get-tuple-element.77, f32[5]{0:T(128)S(1)} %pad_maximum_fusion.3), channel_id=1, replica_groups=mesh['dp'=4,'fsdp'=8] {'dp','fsdp'}, use_global_device_ids=true, to_apply=%region_33.35 | all-reduce | flops 9 | bytes 72 | tf_op jit(solution)/shard_map/psum | solution.py:174
  1122.5 1.1 fusion.97
  1124.8 8.8 reduce-scatter.9.cloned.1.call-done
  1134.5 5.2 all-gather.1
  1140.3 5.5 gather_fusion.1
  1145.8 3.0 bitcast_multiply_fusion
  1148.9 3.7 copy.142
  1152.6 5.5 mul.298
  1158.1 6.7 fusion.91
  1164.8 2.0 copy.161
  (161 shorter events, 24.4 us)
Async XLA Ops:
  7.2 910.1 %copy-start = (f32[5,320,320]{2,1,0:T(8,128)S(1)}, f32[5,320,320]{2,1,0:T(8,128)}, u32[]{:S(2)}) copy-start(f32[5,320,320]{2,1,0:T(8,128)} %param.29) | copy-start | bytes 6144004
  7.2 4.0 copy-start.25
  7.2 38.5 %copy-start.4 = (bf16[256,640]{1,0:T(8,128)(2,1)S(1)}, bf16[256,640]{1,0:T(8,128)(2,1)}, u32[]{:S(2)}) copy-start(bf16[256,640]{1,0:T(8,128)(2,1)} %param.16) | copy-start | bytes 983044
  7.2 229.4 %all-gather.5.cloned.1.call-start = ((), (), s32[]{:S(2)}) async-start(), calls=%async_computation.5 | async-start | bytes 18432000 | tf_op jit(solution)/shard_map/all_gather | solution.py:116
  11.1 544.6 %reduce-scatter.5.cloned.1.call-start = ((), (), s32[]{:S(2)}) async-start(), calls=%async_computation.6 | async-start | bytes 40960000 | tf_op jit(solution)/shard_map/reduce_scatter | solution.py:245
  46.0 198.6 %copy-start.27 = (f32[256]{0:T(256)}, f32[256]{0:T(256)S(1)}, u32[]{:S(2)}) copy-start(f32[256]{0:T(256)S(1)} %fusion.63) | copy-start | bytes 3076
  240.5 5.1 copy-start.12
  241.7 3.9 copy-start.14
  243.8 1.9 copy-start.22
  243.8 3.6 slice-start.2
  244.7 2.7 copy-start.1
  244.7 4.5 slice-start.3
  245.6 4.9 slice-start.4
  245.7 6.0 slice-start.5
  252.5 15.0 %copy-start.16 = (bf16[256,640]{1,0:T(8,128)(2,1)S(1)}, bf16[256,640]{1,0:T(8,128)(2,1)}, u32[]{:S(2)}) copy-start(bf16[256,640]{1,0:T(8,128)(2,1)} %param.17) | copy-start | bytes 983044
  274.1 2.4 copy-start.19
  276.9 0.9 copy-start.6
  282.6 4.1 copy-start.2
  282.6 4.2 copy-start.9
  282.6 4.3 copy-start.23
  286.9 17.8 %copy-start.8 = (bf16[20,32,256]{2,1,0:T(8,128)(2,1)}, bf16[20,32,256]{2,1,0:T(8,128)(2,1)S(1)}, u32[]{:S(2)}) copy-start(bf16[20,32,256]{2,1,0:T(8,128)(2,1)S(1)} %fusion.48) | copy-start | bytes 983044
  288.2 1.4 copy-start.15
  288.2 2.3 copy-start.13
  289.7 1.7 copy-start.20
  290.6 14.1 %copy-start.10 = (bf16[20,32,256]{2,1,0:T(8,128)(2,1)}, bf16[20,32,256]{2,1,0:T(8,128)(2,1)S(1)}, u32[]{:S(2)}) copy-start(bf16[20,32,256]{2,1,0:T(8,128)(2,1)S(1)} %fusion.47) | copy-start | bytes 983044
  291.4 13.3 %copy-start.11 = (bf16[20,32,256]{2,1,0:T(8,128)(2,1)}, bf16[20,32,256]{2,1,0:T(8,128)(2,1)S(1)}, u32[]{:S(2)}) copy-start(bf16[20,32,256]{2,1,0:T(8,128)(2,1)S(1)} %fusion.46) | copy-start | bytes 983044
  291.4 6.7 copy-start.17
  291.4 6.7 copy-start.21
  304.7 3.3 copy-start.5
  329.9 374.9 %copy-start.35 = (s32[40]{0:T(128)S(1)}, s32[40]{0:T(128)}, u32[]{:S(2)}) copy-start(s32[40]{0:T(128)} %param.25) | copy-start | bytes 484
  329.9 374.8 %reduce-scatter.7.cloned.1.call-start = ((), (), s32[]{:S(2)}) async-start(), calls=%async_computation.7 | async-start | bytes 9216000 | tf_op jit(solution)/shard_map/reduce_scatter | solution.py:249
  555.7 183.5 %all-gather.7.cloned.1.call-start = ((), (), s32[]{:S(2)}) async-start(), calls=%async_computation.8 | async-start | bytes 5120000 | tf_op jit(solution)/shard_map/all_gather | solution.py:253
  766.4 114.7 %all-to-all-start = ((f32[8,80,1,5,320]{4,1,3,2,0:T(8,128)}), f32[8,80,1,5,320]{4,1,3,2,0:T(8,128)}, u32[]{:S(2)}, u32[]{:S(2)}) async-start(f32[8,80,1,5,320]{4,1,3,2,0:T(8,128)} %fusion.65), calls=%async_computation.3 | async-start | bytes 9830400 | tf_op jit(solution)/shard_map/all_to_all | solution.py:272
  883.9 71.0 %slice-start = ((s8[8192000]{0:T(1024)(128)(4,1)}), s8[4194304]{0:T(1024)(128)(4,1)S(1)}, s32[]{:S(2)}) async-start(s8[8192000]{0:T(1024)(128)(4,1)} %bitcast.115), calls=%async_computation.10 | async-start | bytes 8388608
  917.2 37.6 %slice-start.1 = ((s8[8192000]{0:T(1024)(128)(4,1)}), s8[3997696]{0:T(1024)(128)(4,1)S(1)}, s32[]{:S(2)}) async-start(s8[8192000]{0:T(1024)(128)(4,1)} %bitcast.115), calls=%async_computation.11 | async-start | bytes 7995392
  986.5 5.0 copy-start.32
  986.5 5.0 copy-start.36
  986.5 153.8 %all-to-all-start.1 = ((f32[8,80,5,320]{3,1,2,0:T(8,128)}), f32[8,80,5,320]{3,1,2,0:T(8,128)}, u32[]{:S(2)}, u32[]{:S(2)}) async-start(f32[8,80,5,320]{3,1,2,0:T(8,128)} %copy.141), calls=%async_computation.4 | async-start | bytes 9830400 | tf_op jit(solution)/shard_map/all_to_all | solution.py:285
  991.3 142.4 %reduce-scatter.9.cloned.1.call-start = ((), (), s32[]{:S(2)}) async-start(), calls=%async_computation.9 | async-start | bytes 368640 | tf_op jit(solution)/shard_map/reduce_scatter | solution.py:250
  993.8 8.3 copy-start.28
  996.4 6.1 copy-start.7
  996.4 6.1 copy-start.18
  1002.0 24.3 %copy-start.34 = (f32[640]{0:T(1024)S(1)}, f32[640]{0:T(1024)}, u32[]{:S(2)}) copy-start(f32[640]{0:T(1024)} %get-tuple-element.66) | copy-start | bytes 7684
  1026.3 6.0 copy-start.31
  1026.3 6.3 copy-start.33
  1026.4 113.3 %copy-start.26 = (f32[80,16]{0,1:T(8,128)S(1)}, f32[80,16]{0,1:T(8,128)}, u32[]{:S(2)}) copy-start(f32[80,16]{0,1:T(8,128)} %param.22) | copy-start | bytes 15364
  1026.4 113.3 %copy-start.29 = (f32[80,16]{0,1:T(8,128)S(1)}, f32[80,16]{0,1:T(8,128)}, u32[]{:S(2)}) copy-start(f32[80,16]{0,1:T(8,128)} %param.23) | copy-start | bytes 15364
  1026.4 113.3 %copy-start.30 = (f32[80,16]{0,1:T(8,128)S(1)}, f32[80,16]{0,1:T(8,128)}, u32[]{:S(2)}) copy-start(f32[80,16]{0,1:T(8,128)} %param.24) | copy-start | bytes 15364
  1032.3 116.6 %copy-start.24 = (bf16[256,640]{1,0:T(8,128)(2,1)}, bf16[256,640]{1,0:T(8,128)(2,1)S(1)}, u32[]{:S(2)}) copy-start(bf16[256,640]{1,0:T(8,128)(2,1)S(1)} %fusion.42) | copy-start | bytes 983044
  1158.1 6.7 copy-start.3
Sparse Core Ops, SparseCore 0:
  11.2 225.3 all-gather.4
  330.0 225.6 reduce-scatter.4
  559.4 145.2 reduce-scatter.6
  706.1 32.9 all-gather.6
  1026.4 107.1 reduce-scatter.8
